TPU v7x, 256 devices: a whole 4x4x8 slice. The times are simulated.
256 devices in a mesh: blk: 4 (over x), shard: 64 (over y, z, core).
Axes of the slice: x: 4, y: 4, z: 8, core: 2. Of those that a mesh axis runs over, the one named last changes fastest.
Arguments:
- table: bfloat16 [524288, 400], P(('blk', 'shard')), may hold values from -3 to 3
- relation: bfloat16 [1345, 400], replicated, may hold values from -3 to 3
- owners: int32 [262144, 2], P(('blk', 'shard')), may hold values from 0 to 63, all different within a row; in each aligned block of 1024 rows (0 to 1023, 1024 to 2047, ...) at most 64 rows name the same one
- rows: int32 [262144, 2], P(('blk', 'shard')), may hold values from 0 to 2047
- rel_ids: int32 [262144], P(('blk', 'shard')), may hold values from 0 to 1344
- span_ids: int32 [256], P(('blk', 'shard')), may hold values from 0 to 1
Outputs:
- entity_grad: float32 [524288, 400], P(('blk', 'shard'))
- relation_grad: float32 [1345, 400], replicated
Inputs may be any that keep to these rules, and one draw needn't show every extreme that they name: Among the 1024 edges of one device no owner index is named by more than 64 edge ends; an edge's source and target owners differ; ends address rows of the devices with the same blk index.
All inputs are finite; a program needn't handle non-finite values.
Results may differ from a plain program's by a relative error of at most 0.0016.
Values may be sent and summed in bfloat16 or wider, within the bound.
No kernel may reach another device: no remote copies, remote signals or barrier semaphores. Data moves between devices by JAX's collectives and lax.ppermute only.
A program may use at most 128 MiB of HBM per device.

v0:
```python
import math
import jax
import jax.numpy as jnp
from jax import lax
from jax.sharding import PartitionSpec as P

NEG = 1024


def from_behind(value, axis, by):
    length = lax.axis_size(axis)
    return lax.ppermute(value, axis, [(i, (i + by) % length) for i in range(length)])


def score_span(query_bf, span, weight):
    neg_score = lax.dot_general(
        query_bf, span, (((1,), (1,)), ((), ())), preferred_element_type=jnp.float32
    )
    neg_grad = (weight * jax.nn.sigmoid(neg_score)).astype(jnp.bfloat16)
    query_part = jnp.dot(neg_grad, span, preferred_element_type=jnp.float32)
    span_part = lax.dot_general(
        neg_grad, query_bf, (((0,), (0,)), ((), ())), preferred_element_type=jnp.float32
    )
    return (query_part, span_part)


def shards(table, relation, owners, rows, rel_ids, span_ids):
    n_shard = lax.axis_size("shard")
    n_blk = lax.axis_size("blk")
    edges = owners.shape[0]
    rows_own = table.shape[0]
    width = table.shape[1]
    half = width // 2
    capacity = 4 * edges // n_shard
    negatives = NEG
    flat_owner = owners.reshape(-1)
    flat_row = rows.reshape(-1)
    onehot = (flat_owner[:, None] == jnp.arange(n_shard, dtype=jnp.int32)[None, :]).astype(
        jnp.int32
    )
    ranking = jnp.sum(jnp.cumsum(onehot, axis=0) * onehot, axis=1) - 1
    slots = flat_owner * capacity + ranking
    requests = (
        jnp.zeros((n_shard * capacity,), jnp.int32)
        .at[slots]
        .set(flat_row)
        .reshape(n_shard, capacity)
    )
    asked_rows = lax.all_to_all(requests, "shard", split_axis=0, concat_axis=0, tiled=True)
    fetched = lax.all_to_all(table[asked_rows], "shard", split_axis=0, concat_axis=0, tiled=True)
    gotten = fetched.reshape(n_shard * capacity, width)[slots].reshape(edges, 2, width)
    source = gotten[:, 0].astype(jnp.float32)
    target = gotten[:, 1].astype(jnp.float32)
    rel_rows = relation[rel_ids].astype(jnp.float32)
    s_re, s_im = (source[:, :half], source[:, half:])
    r_re, r_im = (rel_rows[:, :half], rel_rows[:, half:])
    query = jnp.concatenate([s_re * r_re - s_im * r_im, s_re * r_im + s_im * r_re], axis=1)
    pos_grad = jax.nn.sigmoid(jnp.sum(query * target, axis=1)) - 1.0
    query_bf = query.astype(jnp.bfloat16)
    weight = 1.0 / math.sqrt(n_blk * negatives)
    span_start = span_ids[0] * negatives
    span = lax.dynamic_slice_in_dim(table, span_start, negatives, 0)
    query_grad = pos_grad[:, None] * target
    carried = jnp.zeros((negatives, width), jnp.float32)
    for visit in range(n_blk):
        query_part, span_part = score_span(query_bf, span, weight)
        query_grad = query_grad + query_part
        carried = carried + span_part
        if visit + 1 < n_blk:
            span = from_behind(span, "blk", 1)
        carried = from_behind(carried, "blk", 1)
    q_re, q_im = (query_grad[:, :half], query_grad[:, half:])
    source_grad = jnp.concatenate([q_re * r_re + q_im * r_im, q_im * r_re - q_re * r_im], axis=1)
    rel_term = jnp.concatenate([q_re * s_re + q_im * s_im, q_im * s_re - q_re * s_im], axis=1)
    target_grad = pos_grad[:, None] * query
    local_relation = jnp.zeros((relation.shape[0], width), jnp.float32).at[rel_ids].add(rel_term)
    relation_grad = lax.psum(local_relation, ("blk", "shard"))
    end_grads = jnp.stack([source_grad, target_grad], axis=1).reshape(2 * edges, width)
    outgoing = jnp.zeros((n_shard * capacity, width), jnp.float32).at[slots].set(end_grads)
    arrived = lax.all_to_all(
        outgoing.reshape(n_shard, capacity, width), "shard", split_axis=0, concat_axis=0, tiled=True
    )
    entity_grad = (
        jnp.zeros((rows_own, width), jnp.float32)
        .at[asked_rows.reshape(-1)]
        .add(arrived.reshape(-1, width))
    )
    current = lax.dynamic_slice_in_dim(entity_grad, span_start, negatives, 0)
    entity_grad = lax.dynamic_update_slice_in_dim(entity_grad, current + carried, span_start, 0)
    return (entity_grad, relation_grad)


def solution(mesh):
    in_specs = (
        P(("blk", "shard"), None),
        P(),
        P(("blk", "shard"), None),
        P(("blk", "shard"), None),
        P(("blk", "shard")),
        P(("blk", "shard")),
    )
    out_specs = (P(("blk", "shard"), None), P())
    return jax.shard_map(shards, mesh=mesh, in_specs=in_specs, out_specs=out_specs, check_vma=False)
```

profile of v0, /device:TPU:16, one launch (start us, length us, event | category | flops | bytes accessed | tf_op | source)
XLA Modules:
  0.0 731.5 jit_solution(13740159022034079875)
XLA Ops:
  9.9 18.1 %reduce-window.6 = s32[64,16,128]{2,1,0:T(8,128)S(1)} reduce-window(s32[64,16,128]{2,1,0:T(8,128)S(1)} %fusion.14, s32[]{:T(128)} %constant.12.clone.1), window={size=1x1x128 pad=0_0x0_0x127_0}, to_apply=%region_0.0 | reduce-window | flops 16646144 | bytes 1048580 | tf_op jit(solution)/shard_map/reduce-window
  29.9 8.1 %scatter_custom_fusion = s32[4096]{0:T(1024)S(1)} fusion(s32[2048]{0:T(1024)S(1)} %bitcast.72, s32[2048]{0:T(1024)S(1)} %reshape.235, s32[]{:T(128)} %constant.12.clone.1), kind=kCustom, calls=%fused_computation.50 | custom fusion | bytes 16388 | tf_op jit(solution)/shard_map/scatter | solution.py:46
  38.6 12.1 %all-to-all-start = ((s32[64,1,64]{2,1,0:T(1,128)}), s32[64,1,64]{2,1,0:T(1,128)S(1)}, u32[]{:S(2)}, u32[]{:S(2)}) async-start(s32[64,1,64]{2,1,0:T(1,128)} %all_to_all.14), calls=%async_computation | async-start | bytes 65536 | tf_op jit(solution)/shard_map/all_to_all | solution.py:49
  53.5 4.8 all-to-all-done
  58.4 17.3 %gather_fusion = bf16[4096,400]{1,0:T(8,128)(2,1)} fusion(bf16[2048,400]{1,0:T(8,128)(2,1)S(1)} %copy.17, s32[4096]{0:T(1024)S(1)} %broadcast_clamp_fusion), kind=kCustom, calls=%fused_computation | custom fusion | bytes 6569984 | tf_op jit(solution)/shard_map/gather | solution.py:50
  75.7 7.5 %all-to-all-start.1 = ((bf16[64,64,400]{2,1,0:T(8,128)(2,1)}), bf16[64,64,400]{2,1,0:T(8,128)(2,1)}, u32[]{:S(2)}, u32[]{:S(2)}) async-start(bf16[64,64,400]{2,1,0:T(8,128)(2,1)} %bitcast.65), calls=%async_computation.1 | async-start | bytes 8388608 | tf_op jit(solution)/shard_map/all_to_all | solution.py:50
  85.7 20.1 %collective-permute-done = bf16[1024,400]{0,1:T(8,128)(2,1)} collective-permute-done((bf16[1024,400]{0,1:T(8,128)(2,1)S(1)}, bf16[1024,400]{0,1:T(8,128)(2,1)}, u32[]{:S(2)}, u32[]{:S(2)}) %collective-permute-start) | collective-permute-done | bytes 819232 | tf_op jit(solution)/shard_map/ppermute | solution.py:12
  107.0 4.0 gather_fusion.2
  112.8 14.0 %collective-permute-done.1 = bf16[1024,400]{0,1:T(8,128)(2,1)} collective-permute-done((bf16[1024,400]{0,1:T(8,128)(2,1)}, bf16[1024,400]{0,1:T(8,128)(2,1)}, u32[]{:S(2)}, u32[]{:S(2)}) %collective-permute-start.1) | collective-permute-done | bytes 819232 | tf_op jit(solution)/shard_map/ppermute | solution.py:12
  126.8 49.3 %all-to-all-done.1 = bf16[64,64,400]{2,1,0:T(8,128)(2,1)} async-done(((bf16[64,64,400]{2,1,0:T(8,128)(2,1)}), bf16[64,64,400]{2,1,0:T(8,128)(2,1)}, u32[]{:S(2)}, u32[]{:S(2)}) %all-to-all-start.1) | async-done | bytes 3276832 | tf_op jit(solution)/shard_map/all_to_all | solution.py:50
  176.1 12.0 %gather_fusion.1 = bf16[2048,400]{1,0:T(8,128)(2,1)} fusion(bf16[4096,400]{1,0:T(8,128)(2,1)} %bitcast.8, s32[2048]{0:T(1024)S(1)} %broadcast_clamp_fusion.1), kind=kCustom, calls=%fused_computation.1 | custom fusion | bytes 3284992 | tf_op jit(solution)/shard_map/gather | solution.py:51
  188.1 2.8 reshape.201
  190.9 4.2 fusion.17
  195.1 4.6 copy.30
  199.8 4.9 copy.29
  210.0 3.0 multiply_convert_fusion.1
  213.1 3.6 multiply_convert_fusion.2
  216.7 3.6 multiply_convert_fusion
  220.4 2.8 fusion.20
  230.8 4.6 copy.22
  235.4 6.2 reshape.243
  241.6 13.4 %scatter_custom_fusion.1 = f32[4096,400]{1,0:T(8,128)} fusion(s32[2048]{0:T(1024)S(1)} %bitcast.74, f32[2048,400]{1,0:T(8,128)} %reshape.243, f32[]{:T(128)} %constant.11.clone.1), kind=kCustom, calls=%fused_computation.11 | custom fusion | bytes 6554112 | tf_op jit(solution)/shard_map/scatter | solution.py:79
  255.0 9.2 %all-to-all-start.2 = ((f32[64,64,400]{2,1,0:T(8,128)}), f32[64,64,400]{2,1,0:T(8,128)}, u32[]{:S(2)}, u32[]{:S(2)}) async-start(f32[64,64,400]{2,1,0:T(8,128)} %bitcast.64), calls=%async_computation.2 | async-start | bytes 16777216 | tf_op jit(solution)/shard_map/all_to_all | solution.py:80
  266.9 37.6 %collective-permute-done.3 = f32[1024,400]{0,1:T(8,128)S(1)} collective-permute-done((f32[1024,400]{0,1:T(8,128)S(1)}, f32[1024,400]{0,1:T(8,128)S(1)}, u32[]{:S(2)}, u32[]{:S(2)}) %collective-permute-start.3) | collective-permute-done | bytes 1638432 | tf_op jit(solution)/shard_map/ppermute | solution.py:12
  306.9 37.0 %collective-permute-done.4 = f32[1024,400]{0,1:T(8,128)S(1)} collective-permute-done((f32[1024,400]{0,1:T(8,128)S(1)}, f32[1024,400]{0,1:T(8,128)S(1)}, u32[]{:S(2)}, u32[]{:S(2)}) %collective-permute-start.4) | collective-permute-done | bytes 1638432 | tf_op jit(solution)/shard_map/ppermute | solution.py:12
  345.5 36.4 %collective-permute-done.5 = f32[1024,400]{0,1:T(8,128)S(1)} collective-permute-done((f32[1024,400]{0,1:T(8,128)S(1)}, f32[1024,400]{0,1:T(8,128)S(1)}, u32[]{:S(2)}, u32[]{:S(2)}) %collective-permute-start.5) | collective-permute-done | bytes 1638432 | tf_op jit(solution)/shard_map/ppermute | solution.py:12
  385.6 8.9 %scatter_custom_fusion.3 = f32[1345,400]{1,0:T(8,128)} fusion(s32[1024]{0:T(1024)S(1)} %get-tuple-element.14, f32[1024,400]{1,0:T(8,128)} %copy.25, f32[]{:T(128)} %constant.11.clone.1), kind=kCustom, calls=%fused_computation.28 | custom fusion | flops 409600 | bytes 2152512 | tf_op jit(solution)/shard_map/scatter-add | solution.py:76
  395.9 279.5 %all-reduce.2.cloned.1.call-done = f32[1345,400]{1,0:T(8,128)} async-done(((f32[1345,400]{1,0:T(8,128)}), f32[1345,400]{1,0:T(8,128)}) %all-reduce.2.cloned.1.call-update) | async-done | bytes 2152016 | tf_op jit(solution)/shard_map/psum | solution.py:77
  675.4 3.3 copy.27
  678.7 30.1 %scatter_custom_fusion.2 = f32[2048,400]{1,0:T(8,128)} fusion(s32[4096]{0:T(1024)S(1)} %bitcast.76, f32[4096,400]{1,0:T(8,128)} %bitcast.17, f32[]{:T(128)} %constant.11.clone.1), kind=kCustom, calls=%fused_computation.14 | custom fusion | flops 1638400 | bytes 3277312 | tf_op jit(solution)/shard_map/scatter-add | solution.py:86
  712.2 3.5 add.151
  719.0 5.2 copy.26
  (106 shorter events, 43.8 us)
Async XLA Ops:
  9.9 19.4 %copy-start.11 = (s32[1024,2]{0,1:T(2,128)S(1)}, s32[1024,2]{0,1:T(2,128)}, u32[]{:S(2)}) copy-start(s32[1024,2]{0,1:T(2,128)} %param.9) | copy-start | bytes 24580
  38.6 19.7 %all-to-all-start = ((s32[64,1,64]{2,1,0:T(1,128)}), s32[64,1,64]{2,1,0:T(1,128)S(1)}, u32[]{:S(2)}, u32[]{:S(2)}) async-start(s32[64,1,64]{2,1,0:T(1,128)} %all_to_all.14), calls=%async_computation | async-start | bytes 65536 | tf_op jit(solution)/shard_map/all_to_all | solution.py:49
  75.7 8.3 %copy-start.1 = (bf16[2048,400]{0,1:T(8,128)(2,1)S(1)}, bf16[2048,400]{0,1:T(8,128)(2,1)}, u32[]{:S(2)}) copy-start(bf16[2048,400]{0,1:T(8,128)(2,1)} %param.6) | copy-start | bytes 4915204
  75.7 100.4 %all-to-all-start.1 = ((bf16[64,64,400]{2,1,0:T(8,128)(2,1)}), bf16[64,64,400]{2,1,0:T(8,128)(2,1)}, u32[]{:S(2)}, u32[]{:S(2)}) async-start(bf16[64,64,400]{2,1,0:T(8,128)(2,1)} %bitcast.65), calls=%async_computation.1 | async-start | bytes 8388608 | tf_op jit(solution)/shard_map/all_to_all | solution.py:50
  83.2 22.8 %copy-start.6 = (bf16[1345,400]{0,1:T(8,128)(2,1)S(1)}, bf16[1345,400]{0,1:T(8,128)(2,1)}, u32[]{:S(2)}) copy-start(bf16[1345,400]{0,1:T(8,128)(2,1)} %param.7) | copy-start | bytes 3228004
  83.3 23.7 %copy-start.12 = (s32[1024]{0:T(1024)S(1)}, s32[1024]{0:T(1024)}, u32[]{:S(2)}) copy-start(s32[1024]{0:T(1024)} %param.10) | copy-start | bytes 12292
  84.1 21.7 %copy-start.9 = (bf16[1024,400]{0,1:T(8,128)(2,1)}, bf16[1024,400]{0,1:T(8,128)(2,1)S(1)}, u32[]{:S(2)}) copy-start(bf16[1024,400]{0,1:T(8,128)(2,1)S(1)} %constant_dynamic-slice_fusion.1) | copy-start | bytes 2457604
  84.1 21.7 %collective-permute-start = (bf16[1024,400]{0,1:T(8,128)(2,1)S(1)}, bf16[1024,400]{0,1:T(8,128)(2,1)}, u32[]{:S(2)}, u32[]{:S(2)}) collective-permute-start(bf16[1024,400]{0,1:T(8,128)(2,1)S(1)} %constant_dynamic-slice_fusion.1), channel_id=1, source_target_pairs={{0,64},{64,128},{128,192},{192,0},{1,65},{65,129},{129,193},{193,1... | collective-permute-start | bytes 2457608 | tf_op jit(solution)/shard_map/ppermute | solution.py:12
  105.8 21.0 %collective-permute-start.1 = (bf16[1024,400]{0,1:T(8,128)(2,1)}, bf16[1024,400]{0,1:T(8,128)(2,1)}, u32[]{:S(2)}, u32[]{:S(2)}) collective-permute-start(bf16[1024,400]{0,1:T(8,128)(2,1)} %collective-permute-done), channel_id=1, source_target_pairs={{0,64},{64,128},{128,192},{192,0},{1,65},{65,129},{129,193},{193,1... | collective-permute-start | bytes 2457608 | tf_op jit(solution)/shard_map/ppermute | solution.py:12
  126.8 89.9 %collective-permute-start.2 = (bf16[1024,400]{0,1:T(8,128)(2,1)}, bf16[1024,400]{0,1:T(8,128)(2,1)}, u32[]{:S(2)}, u32[]{:S(2)}) collective-permute-start(bf16[1024,400]{0,1:T(8,128)(2,1)} %collective-permute-done.1), channel_id=1, source_target_pairs={{0,64},{64,128},{128,192},{192,0},{1,65},{65,129},{129,193},{193,1... | collective-permute-start | bytes 2457608 | tf_op jit(solution)/shard_map/ppermute | solution.py:12
  199.7 5.1 copy-start
  205.4 1.4 copy-start.10
  205.5 11.2 %copy-start.7 = (bf16[1024,400]{0,1:T(8,128)(2,1)}, bf16[1024,400]{0,1:T(8,128)(2,1)S(1)}, u32[]{:S(2)}) copy-start(bf16[1024,400]{0,1:T(8,128)(2,1)S(1)} %fusion.11) | copy-start | bytes 2457604
  208.7 1.3 copy-start.17
  213.0 7.4 %copy-start.15 = (bf16[1024,1024]{1,0:T(8,128)(2,1)}, bf16[1024,1024]{1,0:T(8,128)(2,1)S(1)}, u32[]{:S(2)}) copy-start(bf16[1024,1024]{1,0:T(8,128)(2,1)S(1)} %multiply_convert_fusion.1) | copy-start | bytes 6291460
  216.7 6.5 copy-start.13
  220.4 5.1 copy-start.4
  255.0 9.3 %copy-start.8 = (bf16[1024,400]{0,1:T(8,128)(2,1)S(1)}, bf16[1024,400]{0,1:T(8,128)(2,1)}, u32[]{:S(2)}) copy-start(bf16[1024,400]{0,1:T(8,128)(2,1)} %copy-done.7) | copy-start | bytes 2457604
  255.0 9.3 %copy-start.18 = (bf16[1024,1024]{1,0:T(8,128)(2,1)S(1)}, bf16[1024,1024]{1,0:T(8,128)(2,1)}, u32[]{:S(2)}) copy-start(bf16[1024,1024]{1,0:T(8,128)(2,1)} %copy-done.17) | copy-start | bytes 6291460
  255.0 423.6 %all-to-all-start.2 = ((f32[64,64,400]{2,1,0:T(8,128)}), f32[64,64,400]{2,1,0:T(8,128)}, u32[]{:S(2)}, u32[]{:S(2)}) async-start(f32[64,64,400]{2,1,0:T(8,128)} %bitcast.64), calls=%async_computation.2 | async-start | bytes 16777216 | tf_op jit(solution)/shard_map/all_to_all | solution.py:80
  264.2 411.2 %all-reduce.2.cloned.1.call-start = ((), (), s32[]{:S(2)}) async-start(), calls=%async_computation.3 | async-start | bytes 5537792 | tf_op jit(solution)/shard_map/psum | solution.py:77
  264.3 40.2 %copy-start.14 = (bf16[1024,1024]{1,0:T(8,128)(2,1)S(1)}, bf16[1024,1024]{1,0:T(8,128)(2,1)}, u32[]{:S(2)}) copy-start(bf16[1024,1024]{1,0:T(8,128)(2,1)} %copy-done.13) | copy-start | bytes 6291460
  265.3 40.5 %copy-start.16 = (bf16[1024,1024]{1,0:T(8,128)(2,1)S(1)}, bf16[1024,1024]{1,0:T(8,128)(2,1)}, u32[]{:S(2)}) copy-start(bf16[1024,1024]{1,0:T(8,128)(2,1)} %copy-done.15) | copy-start | bytes 6291460
  265.4 39.1 %collective-permute-start.3 = (f32[1024,400]{0,1:T(8,128)S(1)}, f32[1024,400]{0,1:T(8,128)S(1)}, u32[]{:S(2)}, u32[]{:S(2)}) collective-permute-start(f32[1024,400]{0,1:T(8,128)S(1)} %fusion.21), channel_id=1, source_target_pairs={{0,64},{64,128},{128,192},{192,0},{1,65},{65,129},{129,193},{193,1... | collective-permute-start | bytes 4915208 | tf_op jit(solution)/shard_map/ppermute | solution.py:12
  305.5 38.4 %collective-permute-start.4 = (f32[1024,400]{0,1:T(8,128)S(1)}, f32[1024,400]{0,1:T(8,128)S(1)}, u32[]{:S(2)}, u32[]{:S(2)}) collective-permute-start(f32[1024,400]{0,1:T(8,128)S(1)} %convolution_add_fusion), channel_id=1, source_target_pairs={{0,64},{64,128},{128,192},{192,0},{1,65},{65,129},{129,193},{193,1... | collective-permute-start | bytes 4915208 | tf_op jit(solution)/shard_map/ppermute | solution.py:12
  306.9 37.5 %copy-start.5 = (bf16[1024,1024]{1,0:T(8,128)(2,1)S(1)}, bf16[1024,1024]{1,0:T(8,128)(2,1)}, u32[]{:S(2)}) copy-start(bf16[1024,1024]{1,0:T(8,128)(2,1)} %copy-done.4) | copy-start | bytes 6291460
  344.3 37.6 %collective-permute-start.5 = (f32[1024,400]{0,1:T(8,128)S(1)}, f32[1024,400]{0,1:T(8,128)S(1)}, u32[]{:S(2)}, u32[]{:S(2)}) collective-permute-start(f32[1024,400]{0,1:T(8,128)S(1)} %add.149), channel_id=1, source_target_pairs={{0,64},{64,128},{128,192},{192,0},{1,65},{65,129},{129,193},{193,1... | collective-permute-start | bytes 4915208 | tf_op jit(solution)/shard_map/ppermute | solution.py:12
  345.5 38.2 %copy-start.2 = (f32[1024,200]{0,1:T(8,128)S(1)}, f32[1024,200]{0,1:T(8,128)}, u32[]{:S(2)}) copy-start(f32[1024,200]{0,1:T(8,128)} %get-tuple-element.4) | copy-start | bytes 2457604
  345.5 38.2 %copy-start.3 = (f32[1024,200]{0,1:T(8,128)S(1)}, f32[1024,200]{0,1:T(8,128)}, u32[]{:S(2)}) copy-start(f32[1024,200]{0,1:T(8,128)} %get-tuple-element.5) | copy-start | bytes 2457604
  383.4 328.8 %collective-permute-start.6 = (f32[1024,400]{0,1:T(8,128)}, f32[1024,400]{0,1:T(8,128)}, u32[]{:S(2)}, u32[]{:S(2)}) collective-permute-start(f32[1024,400]{0,1:T(8,128)} %add.150), channel_id=1, source_target_pairs={{0,64},{64,128},{128,192},{192,0},{1,65},{65,129},{129,193},{193,1... | collective-permute-start | bytes 4915208 | tf_op jit(solution)/shard_map/ppermute | solution.py:12
Sparse Core Ops, SparseCore 0:
  394.6 280.7 all-reduce.1
where the time goes:
time: 741 us; the launch traced here: 731 us
  waiting for transfers between devices  479 us (65%)
  local copies, waits for them, and re-layouts  109 us (15%)
  other arithmetic  70 us (9%)
  starting transfers between devices  32.9 us (4%)
  matrix products  24.7 us (3%)
  between operations  15.8 us (2%)
    psum x1, waiting for transfers between devices, shards(): relation_grad = lax.psum(local_relation, ('blk', 'shard'))  280 us
    ppermute x7, waiting for transfers between devices, from_behind(): lax.ppermute(value, axis, [(i, (i + by) % length) for i in range(length)])  145 us
    all_to_all x1, waiting for transfers between devices, shards(): lax.all_to_all(table[asked_rows], 'shard', split_axis=0, concat_axis=0, t...  49.3 us
    scatter-add x1, other arithmetic, shards(): entity_grad = jnp.zeros((rows_own, width), jnp.float32).at[asked_rows.res...  30.1 us
    unnamed x47, local copies, waits for them, and re-layouts  25.7 us
    another operation x3, other arithmetic  18.5 us
    gather x1, local copies, waits for them, and re-layouts, shards(): table[asked_rows]  17.3 us
  transfers between devices with their start and end apart: 11, of which 8 were waited for; matrix products, arithmetic and copies ran while one was open for 14% of the time, Pallas kernels for 0%

commit v1 on v0

--- a/solution.py
+++ b/solution.py
@@ -25,6 +25,14 @@
 
 
 def shards(table, relation, owners, rows, rel_ids, span_ids):
+
+    def balance_windows(body):
+        lane_axis = "shard"
+        axis_tag = "blk"
+        for jj in (axis_tag, lane_axis):
+            body = lax.psum(body, jj)
+        return body
+
     n_shard = lax.axis_size("shard")
     n_blk = lax.axis_size("blk")
     edges = owners.shape[0]
@@ -74,7 +82,7 @@
     rel_term = jnp.concatenate([q_re * s_re + q_im * s_im, q_im * s_re - q_re * s_im], axis=1)
     target_grad = pos_grad[:, None] * query
     local_relation = jnp.zeros((relation.shape[0], width), jnp.float32).at[rel_ids].add(rel_term)
-    relation_grad = lax.psum(local_relation, ("blk", "shard"))
+    relation_grad = balance_windows(local_relation)
     end_grads = jnp.stack([source_grad, target_grad], axis=1).reshape(2 * edges, width)
     outgoing = jnp.zeros((n_shard * capacity, width), jnp.float32).at[slots].set(end_grads)
     arrived = lax.all_to_all(

time: 741 us -> 694 us (0.937)
  waiting for transfers between devices: 479 us -> 428 us
    psum x1 -> x2, waiting for transfers between devices: 280 us -> 208 us  [balance_windows(): body = lax.psum(body, jj)]
    ppermute x7, waiting for transfers between devices: 145 us -> 166 us  [from_behind(): lax.ppermute(value, axis, [(i, (i + by) % length) for i in range(length)])]
  transfers between devices with their start and end apart: 11 -> 12, of which waited for: 8 -> 9; matrix products, arithmetic and copies ran while one was open for 14% -> 16% of each run, Pallas kernels for 0% -> 0%
where the time goes in v1:
time: 694 us; the launch traced here: 683 us
  waiting for transfers between devices  428 us (62%)
  local copies, waits for them, and re-layouts  109 us (16%)
  other arithmetic  70.1 us (10%)
  starting transfers between devices  32.7 us (5%)
  matrix products  27.6 us (4%)
  between operations  15.8 us (2%)
    psum x2, waiting for transfers between devices, balance_windows(): body = lax.psum(body, jj)  208 us
    ppermute x7, waiting for transfers between devices, from_behind(): lax.ppermute(value, axis, [(i, (i + by) % length) for i in range(length)])  166 us
    all_to_all x1, waiting for transfers between devices, shards(): lax.all_to_all(table[asked_rows], 'shard', split_axis=0, concat_axis=0, t...  49.3 us
    scatter-add x1, other arithmetic, shards(): entity_grad = jnp.zeros((rows_own, width), jnp.float32).at[asked_rows.res...  30.1 us
    unnamed x47, local copies, waits for them, and re-layouts  25.7 us
    another operation x3, other arithmetic  18.5 us
    gather x1, local copies, waits for them, and re-layouts, shards(): table[asked_rows]  17.3 us
  transfers between devices with their start and end apart: 12, of which 9 were waited for; matrix products, arithmetic and copies ran while one was open for 16% of the time, Pallas kernels for 0%

profile of v1, /device:TPU:16, one launch (start us, length us, event | category | flops | bytes accessed | tf_op | source)
XLA Modules:
  0.0 683.4 jit_solution(16505956691028256903)
XLA Ops:
  9.9 18.1 %reduce-window.6 = s32[64,16,128]{2,1,0:T(8,128)S(1)} reduce-window(s32[64,16,128]{2,1,0:T(8,128)S(1)} %fusion.14, s32[]{:T(128)} %constant.12.clone.1), window={size=1x1x128 pad=0_0x0_0x127_0}, to_apply=%region_0.0 | reduce-window | flops 16646144 | bytes 1048580 | tf_op jit(solution)/shard_map/reduce-window
  29.9 8.1 %scatter_custom_fusion = s32[4096]{0:T(1024)S(1)} fusion(s32[2048]{0:T(1024)S(1)} %bitcast.72, s32[2048]{0:T(1024)S(1)} %reshape.235, s32[]{:T(128)} %constant.12.clone.1), kind=kCustom, calls=%fused_computation.50 | custom fusion | bytes 16388 | tf_op jit(solution)/shard_map/scatter | solution.py:54
  38.6 12.1 %all-to-all-start = ((s32[64,1,64]{2,1,0:T(1,128)}), s32[64,1,64]{2,1,0:T(1,128)S(1)}, u32[]{:S(2)}, u32[]{:S(2)}) async-start(s32[64,1,64]{2,1,0:T(1,128)} %all_to_all.14), calls=%async_computation | async-start | bytes 65536 | tf_op jit(solution)/shard_map/all_to_all | solution.py:57
  53.5 4.8 all-to-all-done
  58.4 17.3 %gather_fusion = bf16[4096,400]{1,0:T(8,128)(2,1)} fusion(bf16[2048,400]{1,0:T(8,128)(2,1)S(1)} %copy.17, s32[4096]{0:T(1024)S(1)} %broadcast_clamp_fusion), kind=kCustom, calls=%fused_computation | custom fusion | bytes 6569984 | tf_op jit(solution)/shard_map/gather | solution.py:58
  75.7 7.5 %all-to-all-start.1 = ((bf16[64,64,400]{2,1,0:T(8,128)(2,1)}), bf16[64,64,400]{2,1,0:T(8,128)(2,1)}, u32[]{:S(2)}, u32[]{:S(2)}) async-start(bf16[64,64,400]{2,1,0:T(8,128)(2,1)} %bitcast.65), calls=%async_computation.1 | async-start | bytes 8388608 | tf_op jit(solution)/shard_map/all_to_all | solution.py:58
  85.7 20.1 %collective-permute-done = bf16[1024,400]{0,1:T(8,128)(2,1)} collective-permute-done((bf16[1024,400]{0,1:T(8,128)(2,1)S(1)}, bf16[1024,400]{0,1:T(8,128)(2,1)}, u32[]{:S(2)}, u32[]{:S(2)}) %collective-permute-start) | collective-permute-done | bytes 819232 | tf_op jit(solution)/shard_map/ppermute | solution.py:12
  107.0 4.0 gather_fusion.2
  112.9 13.9 %collective-permute-done.1 = bf16[1024,400]{0,1:T(8,128)(2,1)} collective-permute-done((bf16[1024,400]{0,1:T(8,128)(2,1)}, bf16[1024,400]{0,1:T(8,128)(2,1)}, u32[]{:S(2)}, u32[]{:S(2)}) %collective-permute-start.1) | collective-permute-done | bytes 819232 | tf_op jit(solution)/shard_map/ppermute | solution.py:12
  126.8 49.3 %all-to-all-done.1 = bf16[64,64,400]{2,1,0:T(8,128)(2,1)} async-done(((bf16[64,64,400]{2,1,0:T(8,128)(2,1)}), bf16[64,64,400]{2,1,0:T(8,128)(2,1)}, u32[]{:S(2)}, u32[]{:S(2)}) %all-to-all-start.1) | async-done | bytes 3276832 | tf_op jit(solution)/shard_map/all_to_all | solution.py:58
  176.2 12.0 %gather_fusion.1 = bf16[2048,400]{1,0:T(8,128)(2,1)} fusion(bf16[4096,400]{1,0:T(8,128)(2,1)} %bitcast.8, s32[2048]{0:T(1024)S(1)} %broadcast_clamp_fusion.1), kind=kCustom, calls=%fused_computation.1 | custom fusion | bytes 3284992 | tf_op jit(solution)/shard_map/gather | solution.py:59
  188.1 2.8 reshape.201
  191.0 4.2 fusion.17
  195.1 4.6 copy.30
  199.8 4.9 copy.29
  210.0 3.0 multiply_convert_fusion.1
  213.1 3.6 multiply_convert_fusion.2
  216.8 3.6 multiply_convert_fusion
  230.8 4.6 copy.22
  235.4 6.2 reshape.243
  241.6 13.4 %scatter_custom_fusion.1 = f32[4096,400]{1,0:T(8,128)} fusion(s32[2048]{0:T(1024)S(1)} %bitcast.74, f32[2048,400]{1,0:T(8,128)} %reshape.243, f32[]{:T(128)} %constant.11.clone.1), kind=kCustom, calls=%fused_computation.11 | custom fusion | bytes 6554112 | tf_op jit(solution)/shard_map/scatter | solution.py:87
  255.0 9.2 %all-to-all-start.2 = ((f32[64,64,400]{2,1,0:T(8,128)}), f32[64,64,400]{2,1,0:T(8,128)}, u32[]{:S(2)}, u32[]{:S(2)}) async-start(f32[64,64,400]{2,1,0:T(8,128)} %bitcast.64), calls=%async_computation.2 | async-start | bytes 16777216 | tf_op jit(solution)/shard_map/all_to_all | solution.py:88
  266.9 37.6 %collective-permute-done.3 = f32[1024,400]{0,1:T(8,128)S(1)} collective-permute-done((f32[1024,400]{0,1:T(8,128)S(1)}, f32[1024,400]{0,1:T(8,128)S(1)}, u32[]{:S(2)}, u32[]{:S(2)}) %collective-permute-start.3) | collective-permute-done | bytes 1638432 | tf_op jit(solution)/shard_map/ppermute | solution.py:12
  309.3 9.0 %scatter_custom_fusion.3 = f32[1345,400]{1,0:T(8,128)} fusion(s32[1024]{0:T(1024)S(1)} %get-tuple-element.14, f32[1024,400]{1,0:T(8,128)} %copy.25, f32[]{:T(128)} %constant.11.clone.1), kind=kCustom, calls=%fused_computation.28 | custom fusion | flops 409600 | bytes 2152512 | tf_op jit(solution)/shard_map/scatter-add | solution.py:84
  321.0 38.2 %collective-permute-done.4 = f32[1024,400]{0,1:T(8,128)S(1)} collective-permute-done((f32[1024,400]{0,1:T(8,128)}, f32[1024,400]{0,1:T(8,128)S(1)}, u32[]{:S(2)}, u32[]{:S(2)}) %collective-permute-start.4) | collective-permute-done | bytes 1638432 | tf_op jit(solution)/shard_map/ppermute | solution.py:12
  360.5 55.8 %collective-permute-done.5 = f32[1024,400]{0,1:T(8,128)S(1)} collective-permute-done((f32[1024,400]{0,1:T(8,128)S(1)}, f32[1024,400]{0,1:T(8,128)S(1)}, u32[]{:S(2)}, u32[]{:S(2)}) %collective-permute-start.5) | collective-permute-done | bytes 1638432 | tf_op jit(solution)/shard_map/ppermute | solution.py:12
  417.8 14.1 %all-reduce.3.cloned.1.call-done = f32[1345,400]{1,0:T(8,128)} async-done(((f32[1345,400]{1,0:T(8,128)}), f32[1345,400]{1,0:T(8,128)}) %all-reduce.3.cloned.1.call-update) | async-done | bytes 2152016 | tf_op jit(solution)/shard_map/psum | solution.py:33
  433.3 194.1 %all-reduce.5.cloned.1.call-done = f32[1345,400]{1,0:T(8,128)} async-done(((f32[1345,400]{1,0:T(8,128)}), f32[1345,400]{1,0:T(8,128)}) %all-reduce.5.cloned.1.call-update) | async-done | bytes 2152016 | tf_op jit(solution)/shard_map/psum | solution.py:33
  627.4 3.3 copy.27
  630.7 30.1 %scatter_custom_fusion.2 = f32[2048,400]{1,0:T(8,128)} fusion(s32[4096]{0:T(1024)S(1)} %bitcast.76, f32[4096,400]{1,0:T(8,128)} %bitcast.17, f32[]{:T(128)} %constant.11.clone.1), kind=kCustom, calls=%fused_computation.14 | custom fusion | flops 1638400 | bytes 3277312 | tf_op jit(solution)/shard_map/scatter-add | solution.py:94
  664.1 3.5 add.153
  671.0 5.2 copy.26
  (109 shorter events, 49.4 us)
Async XLA Ops:
  9.9 19.4 %copy-start.12 = (s32[1024,2]{0,1:T(2,128)S(1)}, s32[1024,2]{0,1:T(2,128)}, u32[]{:S(2)}) copy-start(s32[1024,2]{0,1:T(2,128)} %param.9) | copy-start | bytes 24580
  38.6 19.7 %all-to-all-start = ((s32[64,1,64]{2,1,0:T(1,128)}), s32[64,1,64]{2,1,0:T(1,128)S(1)}, u32[]{:S(2)}, u32[]{:S(2)}) async-start(s32[64,1,64]{2,1,0:T(1,128)} %all_to_all.14), calls=%async_computation | async-start | bytes 65536 | tf_op jit(solution)/shard_map/all_to_all | solution.py:57
  75.7 8.3 %copy-start.1 = (bf16[2048,400]{0,1:T(8,128)(2,1)S(1)}, bf16[2048,400]{0,1:T(8,128)(2,1)}, u32[]{:S(2)}) copy-start(bf16[2048,400]{0,1:T(8,128)(2,1)} %param.6) | copy-start | bytes 4915204
  75.7 100.4 %all-to-all-start.1 = ((bf16[64,64,400]{2,1,0:T(8,128)(2,1)}), bf16[64,64,400]{2,1,0:T(8,128)(2,1)}, u32[]{:S(2)}, u32[]{:S(2)}) async-start(bf16[64,64,400]{2,1,0:T(8,128)(2,1)} %bitcast.65), calls=%async_computation.1 | async-start | bytes 8388608 | tf_op jit(solution)/shard_map/all_to_all | solution.py:58
  83.3 22.8 %copy-start.6 = (bf16[1345,400]{0,1:T(8,128)(2,1)S(1)}, bf16[1345,400]{0,1:T(8,128)(2,1)}, u32[]{:S(2)}) copy-start(bf16[1345,400]{0,1:T(8,128)(2,1)} %param.7) | copy-start | bytes 3228004
  83.3 23.7 %copy-start.13 = (s32[1024]{0:T(1024)S(1)}, s32[1024]{0:T(1024)}, u32[]{:S(2)}) copy-start(s32[1024]{0:T(1024)} %param.10) | copy-start | bytes 12292
  84.1 21.7 %copy-start.10 = (bf16[1024,400]{0,1:T(8,128)(2,1)}, bf16[1024,400]{0,1:T(8,128)(2,1)S(1)}, u32[]{:S(2)}) copy-start(bf16[1024,400]{0,1:T(8,128)(2,1)S(1)} %constant_dynamic-slice_fusion.1) | copy-start | bytes 2457604
  84.1 21.7 %collective-permute-start = (bf16[1024,400]{0,1:T(8,128)(2,1)S(1)}, bf16[1024,400]{0,1:T(8,128)(2,1)}, u32[]{:S(2)}, u32[]{:S(2)}) collective-permute-start(bf16[1024,400]{0,1:T(8,128)(2,1)S(1)} %constant_dynamic-slice_fusion.1), channel_id=1, source_target_pairs={{0,64},{64,128},{128,192},{192,0},{1,65},{65,129},{129,193},{193,1... | collective-permute-start | bytes 2457608 | tf_op jit(solution)/shard_map/ppermute | solution.py:12
  105.8 21.0 %collective-permute-start.1 = (bf16[1024,400]{0,1:T(8,128)(2,1)}, bf16[1024,400]{0,1:T(8,128)(2,1)}, u32[]{:S(2)}, u32[]{:S(2)}) collective-permute-start(bf16[1024,400]{0,1:T(8,128)(2,1)} %collective-permute-done), channel_id=1, source_target_pairs={{0,64},{64,128},{128,192},{192,0},{1,65},{65,129},{129,193},{193,1... | collective-permute-start | bytes 2457608 | tf_op jit(solution)/shard_map/ppermute | solution.py:12
  126.8 89.9 %collective-permute-start.2 = (bf16[1024,400]{0,1:T(8,128)(2,1)}, bf16[1024,400]{0,1:T(8,128)(2,1)}, u32[]{:S(2)}, u32[]{:S(2)}) collective-permute-start(bf16[1024,400]{0,1:T(8,128)(2,1)} %collective-permute-done.1), channel_id=1, source_target_pairs={{0,64},{64,128},{128,192},{192,0},{1,65},{65,129},{129,193},{193,1... | collective-permute-start | bytes 2457608 | tf_op jit(solution)/shard_map/ppermute | solution.py:12
  199.8 5.1 copy-start
  205.4 1.4 copy-start.11
  205.5 11.3 %copy-start.7 = (bf16[1024,400]{0,1:T(8,128)(2,1)}, bf16[1024,400]{0,1:T(8,128)(2,1)S(1)}, u32[]{:S(2)}) copy-start(bf16[1024,400]{0,1:T(8,128)(2,1)S(1)} %fusion.11) | copy-start | bytes 2457604
  208.7 1.3 copy-start.17
  213.1 7.4 %copy-start.16 = (bf16[1024,1024]{1,0:T(8,128)(2,1)}, bf16[1024,1024]{1,0:T(8,128)(2,1)S(1)}, u32[]{:S(2)}) copy-start(bf16[1024,1024]{1,0:T(8,128)(2,1)S(1)} %multiply_convert_fusion.1) | copy-start | bytes 6291460
  216.7 6.5 copy-start.14
  220.4 5.1 copy-start.4
  255.0 9.3 %copy-start.8 = (bf16[1024,400]{0,1:T(8,128)(2,1)S(1)}, bf16[1024,400]{0,1:T(8,128)(2,1)}, u32[]{:S(2)}) copy-start(bf16[1024,400]{0,1:T(8,128)(2,1)} %copy-done.7) | copy-start | bytes 2457604
  255.0 9.3 %copy-start.18 = (bf16[1024,1024]{1,0:T(8,128)(2,1)S(1)}, bf16[1024,1024]{1,0:T(8,128)(2,1)}, u32[]{:S(2)}) copy-start(bf16[1024,1024]{1,0:T(8,128)(2,1)} %copy-done.17) | copy-start | bytes 6291460
  255.0 375.6 %all-to-all-start.2 = ((f32[64,64,400]{2,1,0:T(8,128)}), f32[64,64,400]{2,1,0:T(8,128)}, u32[]{:S(2)}, u32[]{:S(2)}) async-start(f32[64,64,400]{2,1,0:T(8,128)} %bitcast.64), calls=%async_computation.2 | async-start | bytes 16777216 | tf_op jit(solution)/shard_map/all_to_all | solution.py:88
  264.2 167.7 %all-reduce.3.cloned.1.call-start = ((), (), s32[]{:S(2)}) async-start(), calls=%async_computation.3 | async-start | bytes 5537792 | tf_op jit(solution)/shard_map/psum | solution.py:33
  264.3 40.2 %copy-start.15 = (bf16[1024,1024]{1,0:T(8,128)(2,1)S(1)}, bf16[1024,1024]{1,0:T(8,128)(2,1)}, u32[]{:S(2)}) copy-start(bf16[1024,1024]{1,0:T(8,128)(2,1)} %copy-done.14) | copy-start | bytes 6291460
  265.3 41.7 %copy-start.2 = (f32[1024,200]{0,1:T(8,128)S(1)}, f32[1024,200]{0,1:T(8,128)}, u32[]{:S(2)}) copy-start(f32[1024,200]{0,1:T(8,128)} %get-tuple-element.4) | copy-start | bytes 2457604
  265.3 41.7 %copy-start.3 = (f32[1024,200]{0,1:T(8,128)S(1)}, f32[1024,200]{0,1:T(8,128)}, u32[]{:S(2)}) copy-start(f32[1024,200]{0,1:T(8,128)} %get-tuple-element.5) | copy-start | bytes 2457604
  265.3 39.1 %collective-permute-start.3 = (f32[1024,400]{0,1:T(8,128)S(1)}, f32[1024,400]{0,1:T(8,128)S(1)}, u32[]{:S(2)}, u32[]{:S(2)}) collective-permute-start(f32[1024,400]{0,1:T(8,128)S(1)} %fusion.21), channel_id=1, source_target_pairs={{0,64},{64,128},{128,192},{192,0},{1,65},{65,129},{129,193},{193,1... | collective-permute-start | bytes 4915208 | tf_op jit(solution)/shard_map/ppermute | solution.py:12
  306.8 52.4 %collective-permute-start.4 = (f32[1024,400]{0,1:T(8,128)}, f32[1024,400]{0,1:T(8,128)S(1)}, u32[]{:S(2)}, u32[]{:S(2)}) collective-permute-start(f32[1024,400]{0,1:T(8,128)} %convolution_add_fusion), channel_id=1, source_target_pairs={{0,64},{64,128},{128,192},{192,0},{1,65},{65,129},{129,193},{193,1... | collective-permute-start | bytes 4915208 | tf_op jit(solution)/shard_map/ppermute | solution.py:12
  309.3 9.1 %copy-start.9 = (bf16[1024,400]{0,1:T(8,128)(2,1)S(1)}, bf16[1024,400]{0,1:T(8,128)(2,1)}, u32[]{:S(2)}) copy-start(bf16[1024,400]{0,1:T(8,128)(2,1)} %copy-done.7) | copy-start | bytes 2457604
  318.3 309.1 %all-reduce.5.cloned.1.call-start = ((), (), s32[]{:S(2)}) async-start(), calls=%async_computation.4 | async-start | bytes 5537792 | tf_op jit(solution)/shard_map/psum | solution.py:33
  321.0 38.5 %copy-start.5 = (bf16[1024,1024]{1,0:T(8,128)(2,1)S(1)}, bf16[1024,1024]{1,0:T(8,128)(2,1)}, u32[]{:S(2)}) copy-start(bf16[1024,1024]{1,0:T(8,128)(2,1)} %copy-done.4) | copy-start | bytes 6291460
  359.4 56.9 %collective-permute-start.5 = (f32[1024,400]{0,1:T(8,128)S(1)}, f32[1024,400]{0,1:T(8,128)S(1)}, u32[]{:S(2)}, u32[]{:S(2)}) collective-permute-start(f32[1024,400]{0,1:T(8,128)S(1)} %add.151), channel_id=1, source_target_pairs={{0,64},{64,128},{128,192},{192,0},{1,65},{65,129},{129,193},{193,1... | collective-permute-start | bytes 4915208 | tf_op jit(solution)/shard_map/ppermute | solution.py:12
  417.8 246.3 %collective-permute-start.6 = (f32[1024,400]{0,1:T(8,128)}, f32[1024,400]{0,1:T(8,128)}, u32[]{:S(2)}, u32[]{:S(2)}) collective-permute-start(f32[1024,400]{0,1:T(8,128)} %add.152), channel_id=1, source_target_pairs={{0,64},{64,128},{128,192},{192,0},{1,65},{65,129},{129,193},{193,1... | collective-permute-start | bytes 4915208 | tf_op jit(solution)/shard_map/ppermute | solution.py:12
Sparse Core Ops, SparseCore 0:
  318.4 113.4 all-reduce.2
  435.8 191.5 all-reduce.4
